TPU v7x, 512 devices: a whole 4x8x8 slice. The times are simulated.
512 devices in a mesh: req: 64 (over z, x, core), tp: 8 (over y).
Axes of the slice: x: 4, y: 8, z: 8, core: 2. Of those that a mesh axis runs over, the one named last changes fastest.
Arguments:
- queries: bfloat16 [16384, 7168], P('req', 'tp'), may hold values from -200 to 200
- key_value: bfloat16 [2, 16384, 1024], P(None, 'req', 'tp'), may hold values from -8 to 8
- segment: int32 [16384], P('req'), may hold values from 0 to 31, never falling along the last dimension, each value on 1 to 1024 neighbouring positions
- residual: bfloat16 [16384, 7168], P('req', 'tp'), may hold values from -4 to 4
- out_weight: bfloat16 [7168, 7168], P('tp', 'req'), may hold values from -0.0625 to 0.0625
- head_gain: bfloat16 [7168], P('tp'), may hold values from 0.099609375 to 1.8984375
- vocab_weight: bfloat16 [7168, 64000], P('tp', 'req'), may hold values from -0.21875 to 0.21875
Outputs:
- hidden: bfloat16 [16384, 7168], P('req', 'tp')
- key_cache: bfloat16 [16384, 1024], P('req', 'tp')
- last_norm: float32 [32], replicated
- top_logit: float32 [32], replicated
Inputs may be any that keep to these rules, and one draw needn't show every extreme that they name: `segment`: ids never fall; each of the 32 requests has 1 to 1024 tokens, one has exactly 1024.
All inputs are finite; a program needn't handle non-finite values.
Results may differ from a plain program's by a relative error of at most 0.013.
Values may be sent and summed in bfloat16 or wider, within the bound.
No kernel may reach another device: no remote copies, remote signals or barrier semaphores. Data moves between devices by JAX's collectives and lax.ppermute only.
A program may use at most 128 MiB of HBM per device.

v0:
```python
import jax
import jax.numpy as jnp
from jax import lax
from jax.sharding import Mesh, PartitionSpec as P

D = 7168
HD = 128
GROUP = 7
REACH = 4
REQ = ("z", "x", "c")
theta = 5000000.0
eps = 1e-05
masked_score = -1e30


def from_behind(value, axis, steps):
    count = lax.axis_size(axis)
    initial, last = (max(0, -steps), min(count, count - steps))
    return lax.ppermute(value, axis, [(source, source + steps) for source in range(initial, last)])


def butterfly(value, axis, combine):
    count = lax.axis_size(axis)
    stride = 1
    while stride < count:
        other = lax.ppermute(value, axis, [(source, source ^ stride) for source in range(count)])
        value = combine(value, other)
        stride *= 2
    return value


def halving_scatter(value, axis):
    count = lax.axis_size(axis)
    index = lax.axis_index(axis)
    rows, width = (value.shape[1], value.shape[2])
    held = jnp.moveaxis(value, 0, 1)
    bit = 1
    while bit < count:
        mine = index // bit % 2
        pairs = held.reshape(rows, held.shape[1] // 2, 2, width)
        keep = lax.dynamic_index_in_dim(pairs, mine, 2, keepdims=False)
        give = lax.dynamic_index_in_dim(pairs, 1 - mine, 2, keepdims=False)
        moved = lax.ppermute(give, axis, [(source, source ^ bit) for source in range(count)])
        held = (keep.astype(jnp.float32) + moved.astype(jnp.float32)).astype(value.dtype)
        bit *= 2
    return held.reshape(rows, width).astype(jnp.float32)


def rope_tables(positions, width):
    half_width = width // 2
    frequency = theta ** (-(jnp.arange(half_width, dtype=jnp.float32) * 2.0 / width))
    angles = positions[:, None] * frequency[None, :]
    return (jnp.cos(angles), jnp.sin(angles))


def rotate(values, cosine, sine_table):
    half_width = values.shape[-1] // 2
    first_half = values[..., :half_width]
    second_half = values[..., half_width:]
    table_shape = (cosine.shape[0],) + (1,) * (values.ndim - 2) + (half_width,)
    cosine = cosine.reshape(table_shape)
    sine_table = sine_table.reshape(table_shape)
    return jnp.concatenate(
        [
            first_half * cosine - second_half * sine_table,
            second_half * cosine + first_half * sine_table,
        ],
        axis=-1,
    )


def local(queries, key_value, segment, residual, out_weight, head_gain, vocab_weight):
    tok_rows = segment.shape[0]
    heads_kv = key_value.shape[2] // HD
    requests = lax.axis_size(REQ) // 2
    devices_req = lax.axis_size(REQ)
    device = lax.axis_index(REQ)
    request_ids = jnp.arange(requests, dtype=jnp.int32)
    own_kv = key_value
    width = own_kv.shape[2]
    seg_rows = -(-tok_rows // width)
    seg_flat = jnp.pad(segment, (0, seg_rows * width - tok_rows)).astype(jnp.bfloat16)
    packed = jnp.concatenate(
        [own_kv.reshape(2 * tok_rows, width), seg_flat.reshape(seg_rows, width)], axis=0
    )
    parts_kv, parts_seg = ([], [])
    for back in range(REACH, 0, -1):
        got = from_behind(packed, REQ, back)
        parts_kv.append(got[: 2 * tok_rows].reshape(own_kv.shape))
        parts_seg.append(got[2 * tok_rows :].reshape(-1)[:tok_rows].astype(jnp.int32))
    parts_kv.append(own_kv)
    parts_seg.append(segment)
    next_first = from_behind(segment[:1], REQ, -1)
    window = jnp.concatenate(parts_kv, axis=1)
    seg_window = jnp.concatenate(parts_seg, axis=0)
    span = window.shape[1]
    key_index_i = (device - REACH) * tok_rows + jnp.arange(span, dtype=jnp.int32)
    valid = key_index_i >= 0
    same = (seg_window[:, None] == seg_window[None, :]) & valid[None, :]
    start_i = jnp.min(jnp.where(same, key_index_i[None, :], jnp.int32(2**30)), axis=1)
    key_index = key_index_i.astype(jnp.float32)
    win_start = start_i.astype(jnp.float32)
    win_pos = key_index - win_start
    own_start = win_start[span - tok_rows :]
    tok_index = key_index[span - tok_rows :]
    positions = win_pos[span - tok_rows :]
    cosine, sine_table = rope_tables(win_pos, HD)
    rot_keys = rotate(
        window[0].astype(jnp.float32).reshape(span, heads_kv, HD), cosine, sine_table
    ).astype(jnp.bfloat16)
    q_cos, q_sin = (cosine[span - tok_rows :], sine_table[span - tok_rows :])
    rot_query = rotate(
        queries.astype(jnp.float32).reshape(tok_rows, heads_kv, GROUP, HD), q_cos, q_sin
    ).astype(jnp.bfloat16)
    key_cache = rot_keys[span - tok_rows :].reshape(tok_rows, heads_kv * HD)
    key_rows = rot_keys
    value_rows = window[1].reshape(span, heads_kv, HD)
    q_seg = segment
    allowed = (
        (seg_window[None, :] == q_seg[:, None])
        & valid[None, :]
        & (key_index[None, :] <= tok_index[:, None])
    )
    scale = HD ** (-0.5)
    scores_part = (
        jnp.einsum("qhgd,khd->hgqk", rot_query, key_rows, preferred_element_type=jnp.float32)
        * scale
    )
    scores = jnp.where(allowed[None, None], scores_part, masked_score)
    peak = jnp.max(scores, axis=3, keepdims=True)
    weights = jnp.exp(scores - peak)
    total = jnp.sum(weights, axis=3)
    context = jnp.einsum(
        "hgqk,khd->qhgd",
        weights.astype(jnp.bfloat16),
        value_rows,
        preferred_element_type=jnp.float32,
    )
    context = context / jnp.transpose(total, (2, 0, 1))[..., None]
    attended = context.astype(jnp.bfloat16).reshape(tok_rows, heads_kv * GROUP * HD)
    following = jnp.concatenate([segment[1:], next_first])
    is_last_dev = device == devices_req - 1
    is_end = following != segment
    is_end = is_end.at[tok_rows - 1].set(is_end[tok_rows - 1] | is_last_dev)
    select = (is_end[:, None] & (segment[:, None] == request_ids[None, :])).astype(jnp.bfloat16)
    end_rows = lax.dot_general(
        select,
        jnp.concatenate([attended, residual], axis=1),
        (((0,), (0,)), ((), ())),
        preferred_element_type=jnp.float32,
    ).astype(jnp.bfloat16)
    end_rows = butterfly(end_rows, REQ, jnp.add)
    attended, end_rows = lax.optimization_barrier((attended, end_rows))
    end_att, end_res = (end_rows[:, : attended.shape[1]], end_rows[:, attended.shape[1] :])
    groups = lax.axis_size("tp")
    chip_half = lax.all_gather(out_weight, ("z", "x"), axis=1, tiled=True)
    halves = lax.all_gather(chip_half, "c", axis=0, tiled=False)
    cores, k_rows = (halves.shape[0], halves.shape[1])
    per_group = halves.shape[2] // (groups * out_weight.shape[1])
    halves = halves.reshape(cores, k_rows, groups, per_group, out_weight.shape[1])
    both = jnp.einsum(
        "tk,ckgin->gticn",
        jnp.concatenate([attended, end_att], axis=0),
        halves,
        preferred_element_type=jnp.float32,
    ).astype(jnp.bfloat16)
    both = both.reshape(groups, both.shape[1], -1)
    end_part = both[:, tok_rows:]
    end_sum = halving_scatter(end_part, "tp")
    both, end_sum = lax.optimization_barrier((both, end_sum))
    own_share = lax.psum_scatter(both, "tp", scatter_dimension=0, tiled=True)[0, :tok_rows]
    own_share = own_share.astype(jnp.float32)
    hidden = (residual.astype(jnp.float32) + own_share).astype(jnp.bfloat16)
    last_state = (end_res.astype(jnp.float32) + end_sum).astype(jnp.bfloat16).astype(jnp.float32)
    scaled = (last_state * head_gain.astype(jnp.float32)).astype(jnp.bfloat16)
    square_part = jnp.sum(last_state * last_state, axis=1)
    logit_part = jnp.dot(scaled, vocab_weight, preferred_element_type=jnp.float32)
    summed = butterfly(
        jnp.concatenate([logit_part, square_part[:, None]], axis=1).astype(jnp.bfloat16),
        "tp",
        jnp.add,
    ).astype(jnp.float32)
    raw_logits, square_sum = (summed[:, :-1], summed[:, -1])
    mean_square = square_sum / D
    last_norm = jnp.sqrt(mean_square)
    local_top = jnp.max(raw_logits * lax.rsqrt(mean_square + eps)[:, None], axis=1)
    top_logit = butterfly(local_top, REQ, jnp.maximum)
    return (hidden, key_cache, last_norm, top_logit)


def solution(mesh):
    req_size = mesh.shape["req"]
    split = Mesh(mesh.devices.reshape(req_size // 8, 4, 2, mesh.shape["tp"]), REQ + ("tp",))
    placed = (
        P(REQ, "tp"),
        P(None, REQ, "tp"),
        P(REQ),
        P(REQ, "tp"),
        P("tp", REQ),
        P("tp"),
        P("tp", REQ),
    )
    return jax.shard_map(
        local,
        mesh=split,
        in_specs=placed,
        out_specs=(P(REQ, "tp"), P(REQ, "tp"), P(), P()),
        check_vma=False,
    )
```

profile of v0, /device:TPU:56, one launch (start us, length us, event | category | flops | bytes accessed | tf_op | source)
XLA Modules:
  0.0 372.8 jit_solution(6426506884844975606)
XLA Ops:
  8.0 102.5 %all-gather.4.cloned.1.call-done = bf16[896,3584]{0,1:T(8,128)(2,1)} async-done(((bf16[896,112]{0,1:T(8,128)(2,1)}), bf16[896,3584]{0,1:T(8,128)(2,1)}) %all-gather.4.cloned.1.call-update) | async-done | bytes 6422544 | tf_op jit(solution)/shard_map/all_gather | solution.py:156
  112.2 4.0 %collective-permute-start = (bf16[514,128]{1,0:T(8,128)(2,1)S(1)}, bf16[514,128]{1,0:T(8,128)(2,1)}, u32[]{:S(2)}, u32[]{:S(2)}) collective-permute-start(bf16[514,128]{1,0:T(8,128)(2,1)S(1)} %pad_maximum_fusion), channel_id=1, source_target_pairs={{0,32},{8,40},{16,48},{24,56},{32,64},{40,72},{48,80},{56,88},{64,... | collective-permute-start | bytes 394760 | tf_op jit(solution)/shard_map/ppermute | solution.py:19
  116.2 1.9 collective-permute-start.1
  118.1 2.8 collective-permute-start.2
  121.0 4.4 %collective-permute-start.3 = (bf16[514,128]{1,0:T(8,128)(2,1)S(1)}, bf16[514,128]{1,0:T(8,128)(2,1)}, u32[]{:S(2)}, u32[]{:S(2)}) collective-permute-start(bf16[514,128]{1,0:T(8,128)(2,1)S(1)} %pad_maximum_fusion), channel_id=1, source_target_pairs={{0,8},{8,16},{16,24},{24,32},{32,40},{40,48},{48,56},{56,64},{64,7... | collective-permute-start | bytes 394760 | tf_op jit(solution)/shard_map/ppermute | solution.py:19
  125.4 1.2 slice.109
  126.6 1.3 collective-permute-start.4
  128.6 1.3 copy.28
  130.8 1.4 copy.45
  132.2 1.2 copy.44
  135.6 0.9 slice.118
  136.5 0.9 slice.119
  137.4 0.9 slice.120
  142.1 1.6 select_reduce_fusion
  144.4 1.5 fusion.34
  146.0 1.1 compare_and_fusion
  147.1 3.0 fusion.29
  150.1 1.9 fusion.4
  152.0 1.9 fusion.2
  153.9 2.5 fusion.17
  156.6 1.4 convolution_convert_fusion
  158.0 3.0 collective-permute-start.5
  161.1 0.9 collective-permute-done.5
  162.0 2.8 collective-permute-start.6
  164.8 4.5 %collective-permute-done.6 = bf16[32,1792]{1,0:T(8,128)(2,1)S(1)} collective-permute-done((bf16[32,1792]{1,0:T(8,128)(2,1)S(1)}, bf16[32,1792]{1,0:T(8,128)(2,1)S(1)}, u32[]{:S(2)}, u32[]{:S(2)}) %collective-permute-start.6) | collective-permute-done | bytes 114720 | tf_op jit(solution)/shard_map/ppermute | solution.py:26
  169.4 3.6 collective-permute-start.7
  172.9 4.6 %collective-permute-done.7 = bf16[32,1792]{1,0:T(8,128)(2,1)S(1)} collective-permute-done((bf16[32,1792]{1,0:T(8,128)(2,1)S(1)}, bf16[32,1792]{1,0:T(8,128)(2,1)S(1)}, u32[]{:S(2)}, u32[]{:S(2)}) %collective-permute-start.7) | collective-permute-done | bytes 114720 | tf_op jit(solution)/shard_map/ppermute | solution.py:26
  177.6 4.6 %collective-permute-start.8 = (bf16[32,1792]{1,0:T(8,128)(2,1)S(1)}, bf16[32,1792]{1,0:T(8,128)(2,1)S(1)}, u32[]{:S(2)}, u32[]{:S(2)}) collective-permute-start(bf16[32,1792]{1,0:T(8,128)(2,1)S(1)} %add.131), channel_id=1, source_target_pairs={{0,64},{8,72},{16,80},{24,88},{32,96},{40,104},{48,112},{56,120},{... | collective-permute-start | bytes 344072 | tf_op jit(solution)/shard_map/ppermute | solution.py:26
  182.2 2.8 collective-permute-done.8
  184.9 5.0 %collective-permute-start.9 = (bf16[32,1792]{1,0:T(8,128)(2,1)S(1)}, bf16[32,1792]{1,0:T(8,128)(2,1)S(1)}, u32[]{:S(2)}, u32[]{:S(2)}) collective-permute-start(bf16[32,1792]{1,0:T(8,128)(2,1)S(1)} %add.132), channel_id=1, source_target_pairs={{0,128},{8,136},{16,144},{24,152},{32,160},{40,168},{48,176},{56,1... | collective-permute-start | bytes 344072 | tf_op jit(solution)/shard_map/ppermute | solution.py:26
  190.0 2.8 collective-permute-done.9
  192.8 7.6 %collective-permute-start.10 = (bf16[32,1792]{1,0:T(8,128)(2,1)S(1)}, bf16[32,1792]{1,0:T(8,128)(2,1)S(1)}, u32[]{:S(2)}, u32[]{:S(2)}) collective-permute-start(bf16[32,1792]{1,0:T(8,128)(2,1)S(1)} %add.133), channel_id=1, source_target_pairs={{0,256},{8,264},{16,272},{24,280},{32,288},{40,296},{48,304},{56,3... | collective-permute-start | bytes 344072 | tf_op jit(solution)/shard_map/ppermute | solution.py:26
  200.4 3.5 collective-permute-done.10
  204.0 1.0 copy.34
  205.0 24.7 %reshape.392 = bf16[2,896,8,4,112]{1,0,4,3,2:T(2,128)(2,1)} reshape(bf16[1792,3584]{0,1:T(8,128)(2,1)} %all-gather.6.cloned.1.call-done) | data formatting | bytes 25690112 | tf_op jit(solution)/shard_map/reshape | solution.py:160
  229.7 11.9 %convert_bitcast_fusion = bf16[8,288,4,2,112]{4,1,2,0,3:T(8,128)(2,1)} fusion(bf16[2,896,8,4,112]{1,0,4,3,2:T(2,128)(2,1)} %reshape.392, bf16[32,896]{1,0:T(8,128)(2,1)S(1)} %slice.111, bf16[256,896]{1,0:T(8,128)(2,1)S(1)} %copy-done.2), kind=kOutput, calls=%fused_computation.8 | convolution fusion | flops 3702472704 | bytes 17489920 | tf_op jit(solution)/shard_map/tk,ckgin->gticn/dot_general | solution.py:161
  241.6 9.4 %copy.36 = bf16[8,288,4,2,112]{4,3,2,1,0:T(2,128)(2,1)} copy(bf16[8,288,4,2,112]{4,1,2,0,3:T(8,128)(2,1)} %convert_bitcast_fusion) | data formatting | bytes 8257536 | tf_op jit(solution)/shard_map/convert_element_type | solution.py:166
  251.0 15.5 %reshape.393 = bf16[8,288,896]{2,1,0:T(8,128)(2,1)} reshape(bf16[8,288,4,2,112]{4,3,2,1,0:T(2,128)(2,1)} %copy.36) | data formatting | bytes 8257536 | tf_op jit(solution)/shard_map/reshape | solution.py:167
  266.4 1.1 slice.135
  267.5 3.3 collective-permute-start.11
  270.9 4.5 %collective-permute-done.11 = bf16[32,4,896]{2,0,1:T(8,128)(2,1)S(1)} collective-permute-done((bf16[32,4,896]{2,0,1:T(8,128)(2,1)S(1)}, bf16[32,4,896]{2,0,1:T(8,128)(2,1)S(1)}, u32[]{:S(2)}, u32[]{:S(2)}) %collective-permute-start.11) | collective-permute-done | bytes 229408 | tf_op jit(solution)/shard_map/ppermute | solution.py:43
  275.6 5.0 %collective-permute-start.12 = (bf16[32,2,896]{2,0,1:T(8,128)(2,1)S(1)}, bf16[32,2,896]{2,0,1:T(8,128)(2,1)S(1)}, u32[]{:S(2)}, u32[]{:S(2)}) collective-permute-start(bf16[32,2,896]{2,0,1:T(8,128)(2,1)S(1)} %dynamic-slice_bitcast_fusion.1), channel_id=1, source_target_pairs={{0,2},{1,3},{2,0},{3,1},{4,6},{5,7},{6,4},{7,5},{8,10},{9,11},{10,... | collective-permute-start | bytes 344072 | tf_op jit(solution)/shard_map/ppermute | solution.py:43
  280.6 4.6 %collective-permute-done.12 = bf16[32,2,896]{2,0,1:T(8,128)(2,1)S(1)} collective-permute-done((bf16[32,2,896]{2,0,1:T(8,128)(2,1)S(1)}, bf16[32,2,896]{2,0,1:T(8,128)(2,1)S(1)}, u32[]{:S(2)}, u32[]{:S(2)}) %collective-permute-start.12) | collective-permute-done | bytes 114720 | tf_op jit(solution)/shard_map/ppermute | solution.py:43
  285.2 4.3 %collective-permute-start.13 = (bf16[32,1,896]{2,0,1:T(8,128)(2,1)S(1)}, bf16[32,1,896]{2,0,1:T(8,128)(2,1)S(1)}, u32[]{:S(2)}, u32[]{:S(2)}) collective-permute-start(bf16[32,1,896]{2,0,1:T(8,128)(2,1)S(1)} %constant_dynamic-slice_fusion), channel_id=1, source_target_pairs={{0,4},{1,5},{2,6},{3,7},{4,0},{5,1},{6,2},{7,3},{8,12},{9,13},{10,... | collective-permute-start | bytes 172040 | tf_op jit(solution)/shard_map/ppermute | solution.py:43
  289.5 6.0 %collective-permute-done.13 = bf16[32,1,896]{2,0,1:T(8,128)(2,1)S(1)} collective-permute-done((bf16[32,1,896]{2,0,1:T(8,128)(2,1)S(1)}, bf16[32,1,896]{2,0,1:T(8,128)(2,1)S(1)}, u32[]{:S(2)}, u32[]{:S(2)}) %collective-permute-start.13) | collective-permute-done | bytes 57376 | tf_op jit(solution)/shard_map/ppermute | solution.py:43
  296.6 1.9 collective-permute-start.14
  298.5 4.2 %collective-permute-done.14 = bf16[32,1001]{1,0:T(8,128)(2,1)S(1)} collective-permute-done((bf16[32,1001]{1,0:T(8,128)(2,1)S(1)}, bf16[32,1001]{1,0:T(8,128)(2,1)S(1)}, u32[]{:S(2)}, u32[]{:S(2)}) %collective-permute-start.14) | collective-permute-done | bytes 64096 | tf_op jit(solution)/shard_map/ppermute | solution.py:26
  302.8 3.2 collective-permute-start.15
  306.0 4.5 %collective-permute-done.15 = bf16[32,1001]{1,0:T(8,128)(2,1)S(1)} collective-permute-done((bf16[32,1001]{1,0:T(8,128)(2,1)S(1)}, bf16[32,1001]{1,0:T(8,128)(2,1)S(1)}, u32[]{:S(2)}, u32[]{:S(2)}) %collective-permute-start.15) | collective-permute-done | bytes 64096 | tf_op jit(solution)/shard_map/ppermute | solution.py:26
  310.5 6.0 %collective-permute-start.16 = (bf16[32,1001]{1,0:T(8,128)(2,1)S(1)}, bf16[32,1001]{1,0:T(8,128)(2,1)S(1)}, u32[]{:S(2)}, u32[]{:S(2)}) collective-permute-start(bf16[32,1001]{1,0:T(8,128)(2,1)S(1)} %add.150), channel_id=1, source_target_pairs={{0,4},{1,5},{2,6},{3,7},{4,0},{5,1},{6,2},{7,3},{8,12},{9,13},{10,... | collective-permute-start | bytes 192200 | tf_op jit(solution)/shard_map/ppermute | solution.py:26
  316.5 5.8 %collective-permute-done.16 = bf16[32,1001]{1,0:T(8,128)(2,1)S(1)} collective-permute-done((bf16[32,1001]{1,0:T(8,128)(2,1)S(1)}, bf16[32,1001]{1,0:T(8,128)(2,1)S(1)}, u32[]{:S(2)}, u32[]{:S(2)}) %collective-permute-start.16) | collective-permute-done | bytes 64096 | tf_op jit(solution)/shard_map/ppermute | solution.py:26
  323.2 1.9 collective-permute-start.17
  325.1 1.1 collective-permute-done.17
  326.2 2.6 collective-permute-start.18
  328.8 2.8 collective-permute-done.18
  331.6 5.1 %collective-permute-start.19 = (f32[32]{0:T(128)S(1)}, f32[32]{0:T(128)S(1)}, u32[]{:S(2)}, u32[]{:S(2)}) collective-permute-start(f32[32]{0:T(128)S(1)} %max.19), channel_id=1, source_target_pairs={{0,32},{8,40},{16,48},{24,56},{32,0},{40,8},{48,16},{56,24},{64,96... | collective-permute-start | bytes 392 | tf_op jit(solution)/shard_map/ppermute | solution.py:26
  336.7 1.9 collective-permute-done.19
  338.6 3.7 collective-permute-start.20
  342.3 1.7 collective-permute-done.20
  344.0 8.8 %collective-permute-start.21 = (f32[32]{0:T(128)S(1)}, f32[32]{0:T(128)S(1)}, u32[]{:S(2)}, u32[]{:S(2)}) collective-permute-start(f32[32]{0:T(128)S(1)} %max.21), channel_id=1, source_target_pairs={{0,128},{8,136},{16,144},{24,152},{32,160},{40,168},{48,176},{56,1... | collective-permute-start | bytes 392 | tf_op jit(solution)/shard_map/ppermute | solution.py:26
  352.8 1.5 collective-permute-done.21
  354.3 3.4 collective-permute-start.22
  358.5 5.2 %collective-permute-done.22 = f32[32]{0:T(128)S(1)} collective-permute-done((f32[32]{0:T(128)S(1)}, f32[32]{0:T(128)S(1)}, u32[]{:S(2)}, u32[]{:S(2)}) %collective-permute-start.22) | collective-permute-done | bytes 160 | tf_op jit(solution)/shard_map/ppermute | solution.py:26
  364.2 2.0 fusion.23
  (81 shorter events, 13.8 us)
Async XLA Ops:
  7.2 288.7 %copy-start = (bf16[896,1000]{0,1:T(8,128)(2,1)S(1)}, bf16[896,1000]{0,1:T(8,128)(2,1)}, u32[]{:S(2)}) copy-start(bf16[896,1000]{0,1:T(8,128)(2,1)} %param.15) | copy-start | bytes 5376004
  7.2 126.3 %copy-start.3 = (s32[256]{0:T(256)S(1)}, s32[256]{0:T(256)}, u32[]{:S(2)}) copy-start(s32[256]{0:T(256)} %param.11) | copy-start | bytes 3076
  7.2 134.9 %copy-start.1 = (bf16[2,256,128]{2,1,0:T(8,128)(2,1)S(1)}, bf16[2,256,128]{2,1,0:T(8,128)(2,1)}, u32[]{:S(2)}) copy-start(bf16[2,256,128]{2,1,0:T(8,128)(2,1)} %param.10) | copy-start | bytes 393220
  7.2 103.3 %all-gather.4.cloned.1.call-start = ((), (), s32[]{:S(2)}) async-start(), calls=%async_computation.1 | async-start | bytes 6623232 | tf_op jit(solution)/shard_map/all_gather | solution.py:156
  7.9 197.0 %all-gather.6.cloned.1.call-start = ((), (), s32[]{:S(2)}) async-start(), calls=%async_computation.3 | async-start | bytes 19267584 | tf_op jit(solution)/shard_map/all_gather | solution.py:157
  110.6 253.6 %reduce-scatter.2.cloned.1.call-start = ((), (), s32[]{:S(2)}) async-start(), calls=%async_computation.2 | async-start | bytes 4644864 | tf_op jit(solution)/shard_map/reduce_scatter | solution.py:171
  112.2 23.4 %collective-permute-start = (bf16[514,128]{1,0:T(8,128)(2,1)S(1)}, bf16[514,128]{1,0:T(8,128)(2,1)}, u32[]{:S(2)}, u32[]{:S(2)}) collective-permute-start(bf16[514,128]{1,0:T(8,128)(2,1)S(1)} %pad_maximum_fusion), channel_id=1, source_target_pairs={{0,32},{8,40},{16,48},{24,56},{32,64},{40,72},{48,80},{56,88},{64,... | collective-permute-start | bytes 394760 | tf_op jit(solution)/shard_map/ppermute | solution.py:19
  116.2 20.3 %collective-permute-start.1 = (bf16[514,128]{1,0:T(8,128)(2,1)S(1)}, bf16[514,128]{1,0:T(8,128)(2,1)}, u32[]{:S(2)}, u32[]{:S(2)}) collective-permute-start(bf16[514,128]{1,0:T(8,128)(2,1)S(1)} %pad_maximum_fusion), channel_id=1, source_target_pairs={{0,24},{8,32},{16,40},{24,48},{32,56},{40,64},{48,72},{56,80},{64,... | collective-permute-start | bytes 394760 | tf_op jit(solution)/shard_map/ppermute | solution.py:19
  118.1 19.3 %collective-permute-start.2 = (bf16[514,128]{1,0:T(8,128)(2,1)S(1)}, bf16[514,128]{1,0:T(8,128)(2,1)}, u32[]{:S(2)}, u32[]{:S(2)}) collective-permute-start(bf16[514,128]{1,0:T(8,128)(2,1)S(1)} %pad_maximum_fusion), channel_id=1, source_target_pairs={{0,16},{8,24},{16,32},{24,40},{32,48},{40,56},{48,64},{56,72},{64,... | collective-permute-start | bytes 394760 | tf_op jit(solution)/shard_map/ppermute | solution.py:19
  121.0 17.4 %collective-permute-start.3 = (bf16[514,128]{1,0:T(8,128)(2,1)S(1)}, bf16[514,128]{1,0:T(8,128)(2,1)}, u32[]{:S(2)}, u32[]{:S(2)}) collective-permute-start(bf16[514,128]{1,0:T(8,128)(2,1)S(1)} %pad_maximum_fusion), channel_id=1, source_target_pairs={{0,8},{8,16},{16,24},{24,32},{32,40},{40,48},{48,56},{56,64},{64,7... | collective-permute-start | bytes 394760 | tf_op jit(solution)/shard_map/ppermute | solution.py:19
  126.6 6.9 %collective-permute-start.4 = (s32[1]{0:T(128)}, s32[1]{0:T(128)}, u32[]{:S(2)}, u32[]{:S(2)}) collective-permute-start(s32[1]{0:T(128)} %slice.109), channel_id=1, source_target_pairs={{8,0},{16,8},{24,16},{32,24},{40,32},{48,40},{56,48},{64,56},{72,6... | collective-permute-start | bytes 20 | tf_op jit(solution)/shard_map/ppermute | solution.py:19
  158.0 4.0 %collective-permute-start.5 = (bf16[32,1792]{1,0:T(8,128)(2,1)S(1)}, bf16[32,1792]{1,0:T(8,128)(2,1)S(1)}, u32[]{:S(2)}, u32[]{:S(2)}) collective-permute-start(bf16[32,1792]{1,0:T(8,128)(2,1)S(1)} %convolution_convert_fusion), channel_id=1, source_target_pairs={{0,8},{8,0},{16,24},{24,16},{32,40},{40,32},{48,56},{56,48},{64,72... | collective-permute-start | bytes 344072 | tf_op jit(solution)/shard_map/ppermute | solution.py:26
  162.0 7.3 %collective-permute-start.6 = (bf16[32,1792]{1,0:T(8,128)(2,1)S(1)}, bf16[32,1792]{1,0:T(8,128)(2,1)S(1)}, u32[]{:S(2)}, u32[]{:S(2)}) collective-permute-start(bf16[32,1792]{1,0:T(8,128)(2,1)S(1)} %add.129), channel_id=1, source_target_pairs={{0,16},{8,24},{16,0},{24,8},{32,48},{40,56},{48,32},{56,40},{64,80... | collective-permute-start | bytes 344072 | tf_op jit(solution)/shard_map/ppermute | solution.py:26
  169.4 8.2 %collective-permute-start.7 = (bf16[32,1792]{1,0:T(8,128)(2,1)S(1)}, bf16[32,1792]{1,0:T(8,128)(2,1)S(1)}, u32[]{:S(2)}, u32[]{:S(2)}) collective-permute-start(bf16[32,1792]{1,0:T(8,128)(2,1)S(1)} %add.130), channel_id=1, source_target_pairs={{0,32},{8,40},{16,48},{24,56},{32,0},{40,8},{48,16},{56,24},{64,96... | collective-permute-start | bytes 344072 | tf_op jit(solution)/shard_map/ppermute | solution.py:26
  177.6 7.3 %collective-permute-start.8 = (bf16[32,1792]{1,0:T(8,128)(2,1)S(1)}, bf16[32,1792]{1,0:T(8,128)(2,1)S(1)}, u32[]{:S(2)}, u32[]{:S(2)}) collective-permute-start(bf16[32,1792]{1,0:T(8,128)(2,1)S(1)} %add.131), channel_id=1, source_target_pairs={{0,64},{8,72},{16,80},{24,88},{32,96},{40,104},{48,112},{56,120},{... | collective-permute-start | bytes 344072 | tf_op jit(solution)/shard_map/ppermute | solution.py:26
  184.9 7.8 %collective-permute-start.9 = (bf16[32,1792]{1,0:T(8,128)(2,1)S(1)}, bf16[32,1792]{1,0:T(8,128)(2,1)S(1)}, u32[]{:S(2)}, u32[]{:S(2)}) collective-permute-start(bf16[32,1792]{1,0:T(8,128)(2,1)S(1)} %add.132), channel_id=1, source_target_pairs={{0,128},{8,136},{16,144},{24,152},{32,160},{40,168},{48,176},{56,1... | collective-permute-start | bytes 344072 | tf_op jit(solution)/shard_map/ppermute | solution.py:26
  192.8 11.2 %collective-permute-start.10 = (bf16[32,1792]{1,0:T(8,128)(2,1)S(1)}, bf16[32,1792]{1,0:T(8,128)(2,1)S(1)}, u32[]{:S(2)}, u32[]{:S(2)}) collective-permute-start(bf16[32,1792]{1,0:T(8,128)(2,1)S(1)} %add.133), channel_id=1, source_target_pairs={{0,256},{8,264},{16,272},{24,280},{32,288},{40,296},{48,304},{56,3... | collective-permute-start | bytes 344072 | tf_op jit(solution)/shard_map/ppermute | solution.py:26
  205.0 24.7 %copy-start.2 = (bf16[256,896]{1,0:T(8,128)(2,1)S(1)}, bf16[256,896]{1,0:T(8,128)(2,1)}, u32[]{:S(2)}) copy-start(bf16[256,896]{1,0:T(8,128)(2,1)} %copy.34) | copy-start | bytes 1376260
  251.0 44.6 %copy-start.4 = (bf16[896]{0:T(1024)(128)(2,1)S(1)}, bf16[896]{0:T(1024)(128)(2,1)}, u32[]{:S(2)}) copy-start(bf16[896]{0:T(1024)(128)(2,1)} %param.14) | copy-start | bytes 5380
  267.5 7.9 %collective-permute-start.11 = (bf16[32,4,896]{2,0,1:T(8,128)(2,1)S(1)}, bf16[32,4,896]{2,0,1:T(8,128)(2,1)S(1)}, u32[]{:S(2)}, u32[]{:S(2)}) collective-permute-start(bf16[32,4,896]{2,0,1:T(8,128)(2,1)S(1)} %dynamic-slice_bitcast_fusion), channel_id=1, source_target_pairs={{0,1},{1,0},{2,3},{3,2},{4,5},{5,4},{6,7},{7,6},{8,9},{9,8},{10,11... | collective-permute-start | bytes 688136 | tf_op jit(solution)/shard_map/ppermute | solution.py:43
  275.6 9.6 %collective-permute-start.12 = (bf16[32,2,896]{2,0,1:T(8,128)(2,1)S(1)}, bf16[32,2,896]{2,0,1:T(8,128)(2,1)S(1)}, u32[]{:S(2)}, u32[]{:S(2)}) collective-permute-start(bf16[32,2,896]{2,0,1:T(8,128)(2,1)S(1)} %dynamic-slice_bitcast_fusion.1), channel_id=1, source_target_pairs={{0,2},{1,3},{2,0},{3,1},{4,6},{5,7},{6,4},{7,5},{8,10},{9,11},{10,... | collective-permute-start | bytes 344072 | tf_op jit(solution)/shard_map/ppermute | solution.py:43
  285.2 10.4 %collective-permute-start.13 = (bf16[32,1,896]{2,0,1:T(8,128)(2,1)S(1)}, bf16[32,1,896]{2,0,1:T(8,128)(2,1)S(1)}, u32[]{:S(2)}, u32[]{:S(2)}) collective-permute-start(bf16[32,1,896]{2,0,1:T(8,128)(2,1)S(1)} %constant_dynamic-slice_fusion), channel_id=1, source_target_pairs={{0,4},{1,5},{2,6},{3,7},{4,0},{5,1},{6,2},{7,3},{8,12},{9,13},{10,... | collective-permute-start | bytes 172040 | tf_op jit(solution)/shard_map/ppermute | solution.py:43
  296.6 6.2 %collective-permute-start.14 = (bf16[32,1001]{1,0:T(8,128)(2,1)S(1)}, bf16[32,1001]{1,0:T(8,128)(2,1)S(1)}, u32[]{:S(2)}, u32[]{:S(2)}) collective-permute-start(bf16[32,1001]{1,0:T(8,128)(2,1)S(1)} %pad_maximum_fusion.2), channel_id=1, source_target_pairs={{0,1},{1,0},{2,3},{3,2},{4,5},{5,4},{6,7},{7,6},{8,9},{9,8},{10,11... | collective-permute-start | bytes 192200 | tf_op jit(solution)/shard_map/ppermute | solution.py:26
  302.8 7.6 %collective-permute-start.15 = (bf16[32,1001]{1,0:T(8,128)(2,1)S(1)}, bf16[32,1001]{1,0:T(8,128)(2,1)S(1)}, u32[]{:S(2)}, u32[]{:S(2)}) collective-permute-start(bf16[32,1001]{1,0:T(8,128)(2,1)S(1)} %fusion.66), channel_id=1, source_target_pairs={{0,2},{1,3},{2,0},{3,1},{4,6},{5,7},{6,4},{7,5},{8,10},{9,11},{10,... | collective-permute-start | bytes 192200 | tf_op jit(solution)/shard_map/ppermute | solution.py:26
  310.5 11.8 %collective-permute-start.16 = (bf16[32,1001]{1,0:T(8,128)(2,1)S(1)}, bf16[32,1001]{1,0:T(8,128)(2,1)S(1)}, u32[]{:S(2)}, u32[]{:S(2)}) collective-permute-start(bf16[32,1001]{1,0:T(8,128)(2,1)S(1)} %add.150), channel_id=1, source_target_pairs={{0,4},{1,5},{2,6},{3,7},{4,0},{5,1},{6,2},{7,3},{8,12},{9,13},{10,... | collective-permute-start | bytes 192200 | tf_op jit(solution)/shard_map/ppermute | solution.py:26
  323.2 3.0 collective-permute-start.17
  326.2 5.4 %collective-permute-start.18 = (f32[32]{0:T(128)S(1)}, f32[32]{0:T(128)S(1)}, u32[]{:S(2)}, u32[]{:S(2)}) collective-permute-start(f32[32]{0:T(128)S(1)} %max.18), channel_id=1, source_target_pairs={{0,16},{8,24},{16,0},{24,8},{32,48},{40,56},{48,32},{56,40},{64,80... | collective-permute-start | bytes 392 | tf_op jit(solution)/shard_map/ppermute | solution.py:26
  331.6 6.9 %collective-permute-start.19 = (f32[32]{0:T(128)S(1)}, f32[32]{0:T(128)S(1)}, u32[]{:S(2)}, u32[]{:S(2)}) collective-permute-start(f32[32]{0:T(128)S(1)} %max.19), channel_id=1, source_target_pairs={{0,32},{8,40},{16,48},{24,56},{32,0},{40,8},{48,16},{56,24},{64,96... | collective-permute-start | bytes 392 | tf_op jit(solution)/shard_map/ppermute | solution.py:26
  338.6 5.4 %collective-permute-start.20 = (f32[32]{0:T(128)S(1)}, f32[32]{0:T(128)S(1)}, u32[]{:S(2)}, u32[]{:S(2)}) collective-permute-start(f32[32]{0:T(128)S(1)} %max.20), channel_id=1, source_target_pairs={{0,64},{8,72},{16,80},{24,88},{32,96},{40,104},{48,112},{56,120},{... | collective-permute-start | bytes 392 | tf_op jit(solution)/shard_map/ppermute | solution.py:26
  344.0 10.3 %collective-permute-start.21 = (f32[32]{0:T(128)S(1)}, f32[32]{0:T(128)S(1)}, u32[]{:S(2)}, u32[]{:S(2)}) collective-permute-start(f32[32]{0:T(128)S(1)} %max.21), channel_id=1, source_target_pairs={{0,128},{8,136},{16,144},{24,152},{32,160},{40,168},{48,176},{56,1... | collective-permute-start | bytes 392 | tf_op jit(solution)/shard_map/ppermute | solution.py:26
  354.3 9.3 %collective-permute-start.22 = (f32[32]{0:T(128)S(1)}, f32[32]{0:T(128)S(1)}, u32[]{:S(2)}, u32[]{:S(2)}) collective-permute-start(f32[32]{0:T(128)S(1)} %max.22), channel_id=1, source_target_pairs={{0,256},{8,264},{16,272},{24,280},{32,288},{40,296},{48,304},{56,3... | collective-permute-start | bytes 392 | tf_op jit(solution)/shard_map/ppermute | solution.py:26
Sparse Core Ops, SparseCore 0:
  11.2 99.2 all-gather.3
  112.6 29.8 all-gather.5
  295.7 56.9 reduce-scatter.1
where the time goes:
time: 375 us; the launch traced here: 373 us
  waiting for transfers between devices  166 us (44%)
  starting transfers between devices  90.3 us (24%)
  local copies, waits for them, and re-layouts  63.7 us (17%)
  other arithmetic  19.2 us (5%)
  matrix products  18.3 us (5%)
  between operations  15 us (4%)
    all_gather x1, waiting for transfers between devices, local(): chip_half = lax.all_gather(out_weight, ('z', 'x'), axis=1, tiled=True)  103 us
    ppermute x15, starting transfers between devices, butterfly(): lax.ppermute(value, axis, [(source, source ^ stride) for source in range(...  63.1 us
    ppermute x15, waiting for transfers between devices, butterfly(): lax.ppermute(value, axis, [(source, source ^ stride) for source in range(...  47.8 us
    reshape x1, local copies, waits for them, and re-layouts, local(): halves.reshape(cores, k_rows, groups, per_group, out_weight.shape[1])  24.7 us
    reshape x1, local copies, waits for them, and re-layouts, local(): both = both.reshape(groups, both.shape[1], -1)  15.5 us
    ppermute x3, waiting for transfers between devices, halving_scatter(): lax.ppermute(give, axis, [(source, source ^ bit) for source in range(coun...  15.1 us
    ppermute x5, starting transfers between devices, from_behind(): lax.ppermute(value, axis, [(source, source + steps) for source in range(i...  14.4 us
    ppermute x3, starting transfers between devices, halving_scatter(): lax.ppermute(give, axis, [(source, source ^ bit) for source in range(coun...  12.7 us
  transfers between devices with their start and end apart: 26, of which 19 were waited for; matrix products, arithmetic and copies ran while one was open for 10% of the time, Pallas kernels for 0%

commit v1 on v0

--- a/solution.py
+++ b/solution.py
@@ -153,7 +153,10 @@
     attended, end_rows = lax.optimization_barrier((attended, end_rows))
     end_att, end_res = (end_rows[:, : attended.shape[1]], end_rows[:, attended.shape[1] :])
     groups = lax.axis_size("tp")
-    chip_half = lax.all_gather(out_weight, ("z", "x"), axis=1, tiled=True)
+    n_dev = lax.axis_size(("z", "x"))
+    blocks = jnp.stack([out_weight for _ in range(n_dev)])
+    blocks = lax.all_to_all(blocks, ("z", "x"), split_axis=0, concat_axis=0)
+    chip_half = jnp.concatenate(blocks, axis=1)
     halves = lax.all_gather(chip_half, "c", axis=0, tiled=False)
     cores, k_rows = (halves.shape[0], halves.shape[1])
     per_group = halves.shape[2] // (groups * out_weight.shape[1])

time: 375 us -> 426 us (1.14)
  blocking collectives: 0 us -> 158 us
  waiting for transfers between devices: 166 us -> 60 us
    all_to_all x0 -> x1, blocking collectives: none -> 158 us  [local(): blocks = lax.all_to_all(blocks, ('z', 'x'), split_axis=0, concat_axis=0)]
    all_gather x1 -> x0, waiting for transfers between devices: 103 us -> none  [local(): chip_half = lax.all_gather(out_weight, ('z', 'x'), axis=1, tiled=True)]
    reshape x1 -> x0, local copies, waits for them, and re-layouts: 24.7 us -> none  [local(): halves.reshape(cores, k_rows, groups, per_group, out_weight.shape[1])]
    all_gather x0 -> x1, local copies, waits for them, and re-layouts: none -> 18 us  [local(): halves = lax.all_gather(chip_half, 'c', axis=0, tiled=False)]
    another operation x0 -> x2, local copies, waits for them, and re-layouts: none -> 11.1 us  [the longest x1 9.58 us: local(): halves = lax.all_gather(chip_half, 'c', axis=0, tiled=False)]
    ppermute x15, waiting for transfers between devices: 47.8 us -> 43.5 us  [butterfly(): lax.ppermute(value, axis, [(source, source ^ stride) for source in range(...]
  transfers between devices with their start and end apart: 26 -> 25, of which waited for: 19 -> 18; matrix products, arithmetic and copies ran while one was open for 10% -> 8% of each run, Pallas kernels for 0% -> 0%
where the time goes in v1:
time: 426 us; the launch traced here: 423 us
  blocking collectives  158 us (37%)
  starting transfers between devices  89.7 us (21%)
  local copies, waits for them, and re-layouts  65.8 us (15%)
  waiting for transfers between devices  60 us (14%)
  other arithmetic  17.6 us (4%)
  matrix products  16.1 us (4%)
  between operations  15.3 us (4%)
    all_to_all x1, blocking collectives, local(): blocks = lax.all_to_all(blocks, ('z', 'x'), split_axis=0, concat_axis=0)  158 us
    ppermute x15, starting transfers between devices, butterfly(): lax.ppermute(value, axis, [(source, source ^ stride) for source in range(...  63.4 us
    ppermute x15, waiting for transfers between devices, butterfly(): lax.ppermute(value, axis, [(source, source ^ stride) for source in range(...  43.5 us
    all_gather x1, local copies, waits for them, and re-layouts, local(): halves = lax.all_gather(chip_half, 'c', axis=0, tiled=False)  18 us
    ppermute x3, waiting for transfers between devices, halving_scatter(): lax.ppermute(give, axis, [(source, source ^ bit) for source in range(coun...  16.5 us
    reshape x1, local copies, waits for them, and re-layouts, local(): both = both.reshape(groups, both.shape[1], -1)  15.5 us
    ppermute x5, starting transfers between devices, from_behind(): lax.ppermute(value, axis, [(source, source + steps) for source in range(i...  14.5 us
    ppermute x3, starting transfers between devices, halving_scatter(): lax.ppermute(give, axis, [(source, source ^ bit) for source in range(coun...  11.6 us
  transfers between devices with their start and end apart: 25, of which 18 were waited for; matrix products, arithmetic and copies ran while one was open for 8% of the time, Pallas kernels for 0%

profile of v1, /device:TPU:56, one launch (start us, length us, event | category | flops | bytes accessed | tf_op | source)
XLA Modules:
  0.0 422.8 jit_solution(12075701992331295963)
XLA Ops:
  7.2 1.5 stack.2
  8.8 158.4 %all_to_all.5 = bf16[32,896,112]{1,2,0:T(8,128)(2,1)} all-to-all(bf16[32,896,112]{1,2,0:T(8,128)(2,1)S(1)} %stack.2), channel_id=1, replica_groups=mesh['z'=8,'x'=4,'c'=2,'tp'=8] {'z','x'}, dimensions={0} | all-to-all | bytes 12845056 | tf_op jit(solution)/shard_map/all_to_all | solution.py:158
  167.1 9.6 %copy.60 = bf16[1,896,3584]{2,1,0:T(8,128)(2,1)} copy(bf16[1,896,3584]{1,2,0:T(8,128)(2,1)} %bitcast.140) | data formatting | bytes 12845056 | tf_op jit(solution)/shard_map/all_gather;reshape | solution.py:160
  176.8 3.8 collective-permute-start
  180.6 1.9 collective-permute-start.1
  182.6 3.5 collective-permute-start.2
  186.0 4.1 collective-permute-start.3
  190.6 1.3 collective-permute-start.4
  193.1 1.4 copy.71
  194.5 1.3 copy.70
  197.9 0.9 slice.118
  198.9 0.9 slice.119
  199.8 0.9 slice.120
  204.5 1.6 select_reduce_fusion
  206.9 1.5 fusion.30
  208.4 1.1 compare_and_fusion
  209.5 3.0 fusion.25
  212.5 1.9 fusion.2
  214.4 1.9 fusion
  216.3 2.5 fusion.13
  219.0 1.4 convolution_convert_fusion
  220.4 3.0 collective-permute-start.5
  223.4 0.9 collective-permute-done.5
  224.4 2.8 collective-permute-start.6
  227.2 4.5 %collective-permute-done.6 = bf16[32,1792]{1,0:T(8,128)(2,1)S(1)} collective-permute-done((bf16[32,1792]{1,0:T(8,128)(2,1)S(1)}, bf16[32,1792]{1,0:T(8,128)(2,1)S(1)}, u32[]{:S(2)}, u32[]{:S(2)}) %collective-permute-start.6) | collective-permute-done | bytes 114720 | tf_op jit(solution)/shard_map/ppermute | solution.py:26
  231.8 4.2 collective-permute-start.7
  235.9 4.0 collective-permute-done.7
  240.0 4.2 %collective-permute-start.8 = (bf16[32,1792]{1,0:T(8,128)(2,1)S(1)}, bf16[32,1792]{1,0:T(8,128)(2,1)S(1)}, u32[]{:S(2)}, u32[]{:S(2)}) collective-permute-start(bf16[32,1792]{1,0:T(8,128)(2,1)S(1)} %add.131), channel_id=1, source_target_pairs={{0,64},{8,72},{16,80},{24,88},{32,96},{40,104},{48,112},{56,120},{... | collective-permute-start | bytes 344072 | tf_op jit(solution)/shard_map/ppermute | solution.py:26
  244.2 2.8 collective-permute-done.8
  247.0 3.8 collective-permute-start.9
  250.8 3.8 collective-permute-done.9
  254.6 7.0 %collective-permute-start.10 = (bf16[32,1792]{1,0:T(8,128)(2,1)S(1)}, bf16[32,1792]{1,0:T(8,128)(2,1)S(1)}, u32[]{:S(2)}, u32[]{:S(2)}) collective-permute-start(bf16[32,1792]{1,0:T(8,128)(2,1)S(1)} %add.133), channel_id=1, source_target_pairs={{0,256},{8,264},{16,272},{24,280},{32,288},{40,296},{48,304},{56,3... | collective-permute-start | bytes 344072 | tf_op jit(solution)/shard_map/ppermute | solution.py:26
  261.6 3.7 collective-permute-done.10
  265.4 1.0 copy.59
  266.4 18.0 %copy.61 = bf16[2,896,3584]{1,2,0:T(8,128)(2,1)} copy(bf16[2,896,3584]{2,1,0:T(8,128)(2,1)} %all-gather.2.cloned.1.call-done) | data formatting | bytes 25690112 | tf_op jit(solution)/shard_map/all_gather | solution.py:160
  284.4 9.6 %convert_bitcast_fusion = bf16[8,288,4,2,112]{4,1,2,0,3:T(8,128)(2,1)} fusion(bf16[2,896,8,4,112]{1,4,3,2,0:T(8,128)(2,1)} %bitcast.141, bf16[32,896]{1,0:T(8,128)(2,1)S(1)} %slice.111, bf16[256,896]{1,0:T(8,128)(2,1)S(1)} %copy-done.3), kind=kOutput, calls=%fused_computation.6 | convolution fusion | flops 3702472704 | bytes 17489920 | tf_op jit(solution)/shard_map/tk,ckgin->gticn/dot_general | solution.py:164
  294.0 9.4 %copy.62 = bf16[8,288,4,2,112]{4,3,2,1,0:T(2,128)(2,1)} copy(bf16[8,288,4,2,112]{4,1,2,0,3:T(8,128)(2,1)} %convert_bitcast_fusion) | data formatting | bytes 8257536 | tf_op jit(solution)/shard_map/convert_element_type | solution.py:169
  303.4 15.5 %reshape.399 = bf16[8,288,896]{2,1,0:T(8,128)(2,1)} reshape(bf16[8,288,4,2,112]{4,3,2,1,0:T(2,128)(2,1)} %copy.62) | data formatting | bytes 8257536 | tf_op jit(solution)/shard_map/reshape | solution.py:170
  318.9 1.1 slice.135
  320.0 3.3 collective-permute-start.11
  323.3 5.8 %collective-permute-done.11 = bf16[32,4,896]{2,0,1:T(8,128)(2,1)S(1)} collective-permute-done((bf16[32,4,896]{2,0,1:T(8,128)(2,1)S(1)}, bf16[32,4,896]{2,0,1:T(8,128)(2,1)S(1)}, u32[]{:S(2)}, u32[]{:S(2)}) %collective-permute-start.11) | collective-permute-done | bytes 229408 | tf_op jit(solution)/shard_map/ppermute | solution.py:43
  329.2 4.0 collective-permute-start.12
  333.3 5.0 %collective-permute-done.12 = bf16[32,2,896]{2,0,1:T(8,128)(2,1)S(1)} collective-permute-done((bf16[32,2,896]{2,0,1:T(8,128)(2,1)S(1)}, bf16[32,2,896]{2,0,1:T(8,128)(2,1)S(1)}, u32[]{:S(2)}, u32[]{:S(2)}) %collective-permute-start.12) | collective-permute-done | bytes 114720 | tf_op jit(solution)/shard_map/ppermute | solution.py:43
  338.3 4.3 %collective-permute-start.13 = (bf16[32,1,896]{2,0,1:T(8,128)(2,1)S(1)}, bf16[32,1,896]{2,0,1:T(8,128)(2,1)S(1)}, u32[]{:S(2)}, u32[]{:S(2)}) collective-permute-start(bf16[32,1,896]{2,0,1:T(8,128)(2,1)S(1)} %constant_dynamic-slice_fusion), channel_id=1, source_target_pairs={{0,4},{1,5},{2,6},{3,7},{4,0},{5,1},{6,2},{7,3},{8,12},{9,13},{10,... | collective-permute-start | bytes 172040 | tf_op jit(solution)/shard_map/ppermute | solution.py:43
  342.7 5.6 %collective-permute-done.13 = bf16[32,1,896]{2,0,1:T(8,128)(2,1)S(1)} collective-permute-done((bf16[32,1,896]{2,0,1:T(8,128)(2,1)S(1)}, bf16[32,1,896]{2,0,1:T(8,128)(2,1)S(1)}, u32[]{:S(2)}, u32[]{:S(2)}) %collective-permute-start.13) | collective-permute-done | bytes 57376 | tf_op jit(solution)/shard_map/ppermute | solution.py:43
  349.4 2.3 collective-permute-start.14
  351.6 3.9 collective-permute-done.14
  355.6 3.9 collective-permute-start.15
  359.5 3.1 collective-permute-done.15
  362.7 6.2 %collective-permute-start.16 = (bf16[32,1001]{1,0:T(8,128)(2,1)S(1)}, bf16[32,1001]{1,0:T(8,128)(2,1)S(1)}, u32[]{:S(2)}, u32[]{:S(2)}) collective-permute-start(bf16[32,1001]{1,0:T(8,128)(2,1)S(1)} %add.150), channel_id=1, source_target_pairs={{0,4},{1,5},{2,6},{3,7},{4,0},{5,1},{6,2},{7,3},{8,12},{9,13},{10,... | collective-permute-start | bytes 192200 | tf_op jit(solution)/shard_map/ppermute | solution.py:26
  368.9 5.7 %collective-permute-done.16 = bf16[32,1001]{1,0:T(8,128)(2,1)S(1)} collective-permute-done((bf16[32,1001]{1,0:T(8,128)(2,1)S(1)}, bf16[32,1001]{1,0:T(8,128)(2,1)S(1)}, u32[]{:S(2)}, u32[]{:S(2)}) %collective-permute-start.16) | collective-permute-done | bytes 64096 | tf_op jit(solution)/shard_map/ppermute | solution.py:26
  375.4 1.9 collective-permute-start.17
  377.4 1.1 collective-permute-done.17
  378.5 2.9 collective-permute-start.18
  381.4 2.5 collective-permute-done.18
  383.9 6.9 %collective-permute-start.19 = (f32[32]{0:T(128)S(1)}, f32[32]{0:T(128)S(1)}, u32[]{:S(2)}, u32[]{:S(2)}) collective-permute-start(f32[32]{0:T(128)S(1)} %max.19), channel_id=1, source_target_pairs={{0,32},{8,40},{16,48},{24,56},{32,0},{40,8},{48,16},{56,24},{64,96... | collective-permute-start | bytes 392 | tf_op jit(solution)/shard_map/ppermute | solution.py:26
  390.8 1.5 collective-permute-done.19
  392.3 3.3 collective-permute-start.20
  395.6 2.1 collective-permute-done.20
  397.7 4.8 %collective-permute-start.21 = (f32[32]{0:T(128)S(1)}, f32[32]{0:T(128)S(1)}, u32[]{:S(2)}, u32[]{:S(2)}) collective-permute-start(f32[32]{0:T(128)S(1)} %max.21), channel_id=1, source_target_pairs={{0,128},{8,136},{16,144},{24,152},{32,160},{40,168},{48,176},{56,1... | collective-permute-start | bytes 392 | tf_op jit(solution)/shard_map/ppermute | solution.py:26
  402.5 1.5 collective-permute-done.21
  404.1 6.3 %collective-permute-start.22 = (f32[32]{0:T(128)S(1)}, f32[32]{0:T(128)S(1)}, u32[]{:S(2)}, u32[]{:S(2)}) collective-permute-start(f32[32]{0:T(128)S(1)} %max.22), channel_id=1, source_target_pairs={{0,256},{8,264},{16,272},{24,280},{32,288},{40,296},{48,304},{56,3... | collective-permute-start | bytes 392 | tf_op jit(solution)/shard_map/ppermute | solution.py:26
  411.1 2.3 collective-permute-done.22
  413.9 2.0 fusion.19
  (83 shorter events, 11.7 us)
Async XLA Ops:
  7.2 341.5 %copy-start = (bf16[896,1000]{0,1:T(8,128)(2,1)S(1)}, bf16[896,1000]{0,1:T(8,128)(2,1)}, u32[]{:S(2)}) copy-start(bf16[896,1000]{0,1:T(8,128)(2,1)} %param.15) | copy-start | bytes 5376004
  7.2 259.2 %all-gather.2.cloned.1.call-start = ((), (), s32[]{:S(2)}) async-start(), calls=%async_computation.2 | async-start | bytes 19267584 | tf_op jit(solution)/shard_map/all_gather | solution.py:160
  167.1 9.7 %copy-start.4 = (s32[256]{0:T(256)S(1)}, s32[256]{0:T(256)}, u32[]{:S(2)}) copy-start(s32[256]{0:T(256)} %param.11) | copy-start | bytes 3076
  167.1 9.7 %copy-start.1 = (bf16[2,256,128]{2,1,0:T(8,128)(2,1)S(1)}, bf16[2,256,128]{2,1,0:T(8,128)(2,1)}, u32[]{:S(2)}) copy-start(bf16[2,256,128]{2,1,0:T(8,128)(2,1)} %param.10) | copy-start | bytes 393220
  176.7 15.3 %copy-start.2 = (bf16[256,896]{1,0:T(8,128)(2,1)S(1)}, bf16[256,896]{1,0:T(8,128)(2,1)}, u32[]{:S(2)}) copy-start(bf16[256,896]{1,0:T(8,128)(2,1)} %param.9) | copy-start | bytes 1376260
  176.7 237.1 %reduce-scatter.2.cloned.1.call-start = ((), (), s32[]{:S(2)}) async-start(), calls=%async_computation.3 | async-start | bytes 4644864 | tf_op jit(solution)/shard_map/reduce_scatter | solution.py:174
  176.8 21.1 %collective-permute-start = (bf16[514,128]{1,0:T(8,128)(2,1)S(1)}, bf16[514,128]{1,0:T(8,128)(2,1)}, u32[]{:S(2)}, u32[]{:S(2)}) collective-permute-start(bf16[514,128]{1,0:T(8,128)(2,1)S(1)} %pad_maximum_fusion), channel_id=1, source_target_pairs={{0,32},{8,40},{16,48},{24,56},{32,64},{40,72},{48,80},{56,88},{64,... | collective-permute-start | bytes 394760 | tf_op jit(solution)/shard_map/ppermute | solution.py:19
  180.6 18.2 %collective-permute-start.1 = (bf16[514,128]{1,0:T(8,128)(2,1)S(1)}, bf16[514,128]{1,0:T(8,128)(2,1)}, u32[]{:S(2)}, u32[]{:S(2)}) collective-permute-start(bf16[514,128]{1,0:T(8,128)(2,1)S(1)} %pad_maximum_fusion), channel_id=1, source_target_pairs={{0,24},{8,32},{16,40},{24,48},{32,56},{40,64},{48,72},{56,80},{64,... | collective-permute-start | bytes 394760 | tf_op jit(solution)/shard_map/ppermute | solution.py:19
  182.6 17.2 %collective-permute-start.2 = (bf16[514,128]{1,0:T(8,128)(2,1)S(1)}, bf16[514,128]{1,0:T(8,128)(2,1)}, u32[]{:S(2)}, u32[]{:S(2)}) collective-permute-start(bf16[514,128]{1,0:T(8,128)(2,1)S(1)} %pad_maximum_fusion), channel_id=1, source_target_pairs={{0,16},{8,24},{16,32},{24,40},{32,48},{40,56},{48,64},{56,72},{64,... | collective-permute-start | bytes 394760 | tf_op jit(solution)/shard_map/ppermute | solution.py:19
  186.0 14.7 %collective-permute-start.3 = (bf16[514,128]{1,0:T(8,128)(2,1)S(1)}, bf16[514,128]{1,0:T(8,128)(2,1)}, u32[]{:S(2)}, u32[]{:S(2)}) collective-permute-start(bf16[514,128]{1,0:T(8,128)(2,1)S(1)} %pad_maximum_fusion), channel_id=1, source_target_pairs={{0,8},{8,16},{16,24},{24,32},{32,40},{40,48},{48,56},{56,64},{64,7... | collective-permute-start | bytes 394760 | tf_op jit(solution)/shard_map/ppermute | solution.py:19
  190.6 5.1 %collective-permute-start.4 = (s32[1]{0:T(128)}, s32[1]{0:T(128)}, u32[]{:S(2)}, u32[]{:S(2)}) collective-permute-start(s32[1]{0:T(128)} %slice.109), channel_id=1, source_target_pairs={{8,0},{16,8},{24,16},{32,24},{40,32},{48,40},{56,48},{64,56},{72,6... | collective-permute-start | bytes 20 | tf_op jit(solution)/shard_map/ppermute | solution.py:19
  220.4 3.9 collective-permute-start.5
  224.4 7.3 %collective-permute-start.6 = (bf16[32,1792]{1,0:T(8,128)(2,1)S(1)}, bf16[32,1792]{1,0:T(8,128)(2,1)S(1)}, u32[]{:S(2)}, u32[]{:S(2)}) collective-permute-start(bf16[32,1792]{1,0:T(8,128)(2,1)S(1)} %add.129), channel_id=1, source_target_pairs={{0,16},{8,24},{16,0},{24,8},{32,48},{40,56},{48,32},{56,40},{64,80... | collective-permute-start | bytes 344072 | tf_op jit(solution)/shard_map/ppermute | solution.py:26
  231.8 8.2 %collective-permute-start.7 = (bf16[32,1792]{1,0:T(8,128)(2,1)S(1)}, bf16[32,1792]{1,0:T(8,128)(2,1)S(1)}, u32[]{:S(2)}, u32[]{:S(2)}) collective-permute-start(bf16[32,1792]{1,0:T(8,128)(2,1)S(1)} %add.130), channel_id=1, source_target_pairs={{0,32},{8,40},{16,48},{24,56},{32,0},{40,8},{48,16},{56,24},{64,96... | collective-permute-start | bytes 344072 | tf_op jit(solution)/shard_map/ppermute | solution.py:26
  240.0 7.0 %collective-permute-start.8 = (bf16[32,1792]{1,0:T(8,128)(2,1)S(1)}, bf16[32,1792]{1,0:T(8,128)(2,1)S(1)}, u32[]{:S(2)}, u32[]{:S(2)}) collective-permute-start(bf16[32,1792]{1,0:T(8,128)(2,1)S(1)} %add.131), channel_id=1, source_target_pairs={{0,64},{8,72},{16,80},{24,88},{32,96},{40,104},{48,112},{56,120},{... | collective-permute-start | bytes 344072 | tf_op jit(solution)/shard_map/ppermute | solution.py:26
  247.0 7.6 %collective-permute-start.9 = (bf16[32,1792]{1,0:T(8,128)(2,1)S(1)}, bf16[32,1792]{1,0:T(8,128)(2,1)S(1)}, u32[]{:S(2)}, u32[]{:S(2)}) collective-permute-start(bf16[32,1792]{1,0:T(8,128)(2,1)S(1)} %add.132), channel_id=1, source_target_pairs={{0,128},{8,136},{16,144},{24,152},{32,160},{40,168},{48,176},{56,1... | collective-permute-start | bytes 344072 | tf_op jit(solution)/shard_map/ppermute | solution.py:26
  254.6 10.7 %collective-permute-start.10 = (bf16[32,1792]{1,0:T(8,128)(2,1)S(1)}, bf16[32,1792]{1,0:T(8,128)(2,1)S(1)}, u32[]{:S(2)}, u32[]{:S(2)}) collective-permute-start(bf16[32,1792]{1,0:T(8,128)(2,1)S(1)} %add.133), channel_id=1, source_target_pairs={{0,256},{8,264},{16,272},{24,280},{32,288},{40,296},{48,304},{56,3... | collective-permute-start | bytes 344072 | tf_op jit(solution)/shard_map/ppermute | solution.py:26
  266.4 18.0 %copy-start.3 = (bf16[256,896]{1,0:T(8,128)(2,1)S(1)}, bf16[256,896]{1,0:T(8,128)(2,1)}, u32[]{:S(2)}) copy-start(bf16[256,896]{1,0:T(8,128)(2,1)} %copy.59) | copy-start | bytes 1376260
  303.4 45.0 %copy-start.5 = (bf16[896]{0:T(1024)(128)(2,1)S(1)}, bf16[896]{0:T(1024)(128)(2,1)}, u32[]{:S(2)}) copy-start(bf16[896]{0:T(1024)(128)(2,1)} %param.14) | copy-start | bytes 5380
  320.0 9.1 %collective-permute-start.11 = (bf16[32,4,896]{2,0,1:T(8,128)(2,1)S(1)}, bf16[32,4,896]{2,0,1:T(8,128)(2,1)S(1)}, u32[]{:S(2)}, u32[]{:S(2)}) collective-permute-start(bf16[32,4,896]{2,0,1:T(8,128)(2,1)S(1)} %dynamic-slice_bitcast_fusion), channel_id=1, source_target_pairs={{0,1},{1,0},{2,3},{3,2},{4,5},{5,4},{6,7},{7,6},{8,9},{9,8},{10,11... | collective-permute-start | bytes 688136 | tf_op jit(solution)/shard_map/ppermute | solution.py:43
  329.2 9.1 %collective-permute-start.12 = (bf16[32,2,896]{2,0,1:T(8,128)(2,1)S(1)}, bf16[32,2,896]{2,0,1:T(8,128)(2,1)S(1)}, u32[]{:S(2)}, u32[]{:S(2)}) collective-permute-start(bf16[32,2,896]{2,0,1:T(8,128)(2,1)S(1)} %dynamic-slice_bitcast_fusion.1), channel_id=1, source_target_pairs={{0,2},{1,3},{2,0},{3,1},{4,6},{5,7},{6,4},{7,5},{8,10},{9,11},{10,... | collective-permute-start | bytes 344072 | tf_op jit(solution)/shard_map/ppermute | solution.py:43
  338.3 10.0 %collective-permute-start.13 = (bf16[32,1,896]{2,0,1:T(8,128)(2,1)S(1)}, bf16[32,1,896]{2,0,1:T(8,128)(2,1)S(1)}, u32[]{:S(2)}, u32[]{:S(2)}) collective-permute-start(bf16[32,1,896]{2,0,1:T(8,128)(2,1)S(1)} %constant_dynamic-slice_fusion), channel_id=1, source_target_pairs={{0,4},{1,5},{2,6},{3,7},{4,0},{5,1},{6,2},{7,3},{8,12},{9,13},{10,... | collective-permute-start | bytes 172040 | tf_op jit(solution)/shard_map/ppermute | solution.py:43
  349.4 6.2 %collective-permute-start.14 = (bf16[32,1001]{1,0:T(8,128)(2,1)S(1)}, bf16[32,1001]{1,0:T(8,128)(2,1)S(1)}, u32[]{:S(2)}, u32[]{:S(2)}) collective-permute-start(bf16[32,1001]{1,0:T(8,128)(2,1)S(1)} %pad_maximum_fusion.2), channel_id=1, source_target_pairs={{0,1},{1,0},{2,3},{3,2},{4,5},{5,4},{6,7},{7,6},{8,9},{9,8},{10,11... | collective-permute-start | bytes 192200 | tf_op jit(solution)/shard_map/ppermute | solution.py:26
  355.6 7.1 %collective-permute-start.15 = (bf16[32,1001]{1,0:T(8,128)(2,1)S(1)}, bf16[32,1001]{1,0:T(8,128)(2,1)S(1)}, u32[]{:S(2)}, u32[]{:S(2)}) collective-permute-start(bf16[32,1001]{1,0:T(8,128)(2,1)S(1)} %fusion.63), channel_id=1, source_target_pairs={{0,2},{1,3},{2,0},{3,1},{4,6},{5,7},{6,4},{7,5},{8,10},{9,11},{10,... | collective-permute-start | bytes 192200 | tf_op jit(solution)/shard_map/ppermute | solution.py:26
  362.7 11.9 %collective-permute-start.16 = (bf16[32,1001]{1,0:T(8,128)(2,1)S(1)}, bf16[32,1001]{1,0:T(8,128)(2,1)S(1)}, u32[]{:S(2)}, u32[]{:S(2)}) collective-permute-start(bf16[32,1001]{1,0:T(8,128)(2,1)S(1)} %add.150), channel_id=1, source_target_pairs={{0,4},{1,5},{2,6},{3,7},{4,0},{5,1},{6,2},{7,3},{8,12},{9,13},{10,... | collective-permute-start | bytes 192200 | tf_op jit(solution)/shard_map/ppermute | solution.py:26
  375.4 3.0 collective-permute-start.17
  378.5 5.4 %collective-permute-start.18 = (f32[32]{0:T(128)S(1)}, f32[32]{0:T(128)S(1)}, u32[]{:S(2)}, u32[]{:S(2)}) collective-permute-start(f32[32]{0:T(128)S(1)} %max.18), channel_id=1, source_target_pairs={{0,16},{8,24},{16,0},{24,8},{32,48},{40,56},{48,32},{56,40},{64,80... | collective-permute-start | bytes 392 | tf_op jit(solution)/shard_map/ppermute | solution.py:26
  383.9 8.4 %collective-permute-start.19 = (f32[32]{0:T(128)S(1)}, f32[32]{0:T(128)S(1)}, u32[]{:S(2)}, u32[]{:S(2)}) collective-permute-start(f32[32]{0:T(128)S(1)} %max.19), channel_id=1, source_target_pairs={{0,32},{8,40},{16,48},{24,56},{32,0},{40,8},{48,16},{56,24},{64,96... | collective-permute-start | bytes 392 | tf_op jit(solution)/shard_map/ppermute | solution.py:26
  392.3 5.4 %collective-permute-start.20 = (f32[32]{0:T(128)S(1)}, f32[32]{0:T(128)S(1)}, u32[]{:S(2)}, u32[]{:S(2)}) collective-permute-start(f32[32]{0:T(128)S(1)} %max.20), channel_id=1, source_target_pairs={{0,64},{8,72},{16,80},{24,88},{32,96},{40,104},{48,112},{56,120},{... | collective-permute-start | bytes 392 | tf_op jit(solution)/shard_map/ppermute | solution.py:26
  397.7 6.3 %collective-permute-start.21 = (f32[32]{0:T(128)S(1)}, f32[32]{0:T(128)S(1)}, u32[]{:S(2)}, u32[]{:S(2)}) collective-permute-start(f32[32]{0:T(128)S(1)} %max.21), channel_id=1, source_target_pairs={{0,128},{8,136},{16,144},{24,152},{32,160},{40,168},{48,176},{56,1... | collective-permute-start | bytes 392 | tf_op jit(solution)/shard_map/ppermute | solution.py:26
  404.1 9.3 %collective-permute-start.22 = (f32[32]{0:T(128)S(1)}, f32[32]{0:T(128)S(1)}, u32[]{:S(2)}, u32[]{:S(2)}) collective-permute-start(f32[32]{0:T(128)S(1)} %max.22), channel_id=1, source_target_pairs={{0,256},{8,264},{16,272},{24,280},{32,288},{40,296},{48,304},{56,3... | collective-permute-start | bytes 392 | tf_op jit(solution)/shard_map/ppermute | solution.py:26
Sparse Core Ops, SparseCore 0:
  176.9 27.6 all-gather.1
  348.5 55.3 reduce-scatter.1
